TPU v7x, 512 devices: a whole 4x8x8 slice. The times are simulated.
512 devices in a mesh: wide: 32 (over z, x), tensor: 16 (over y, core).
Axes of the slice: x: 4, y: 8, z: 8, core: 2. Of those that a mesh axis runs over, the one named last changes fastest.
Arguments:
- tokens: bfloat16 [16384, 8192], P('wide', 'tensor'), may hold values from -6 to 6
- key_value_weight: bfloat16 [8192, 2048], P(None, 'tensor'), may hold values from -0.0625 to 0.0625
- adapter_down_maps: bfloat16 [8192, 512, 64], P('tensor', 'wide'), may hold values from -0.0625 to 0.0625
- adapter_up_maps: bfloat16 [512, 64, 2048], P('wide', None, 'tensor'), may hold values from -0.75 to 0.75
- adapter_per_row: int32 [16384], P('wide'), may hold values from 0 to 511, as said below
- adapter_storage_slot: int32 [512], replicated, may hold values from 0 to 511, as said below
Outputs:
- kv_out: bfloat16 [16384, 2048], P('wide', 'tensor')
Inputs may be any that keep to these rules, and one draw needn't show every extreme that they name: `adapter_per_row`: the adapter stored at position p belongs to owner p // 16 of wide. Among the 512 rows of one index of wide, at most 32 name adapters of one owner; in every draw one owner gets exactly 32 rows from every index of wide. `adapter_storage_slot`: each position is taken by exactly one adapter.
All inputs are finite; a program needn't handle non-finite values.
Results may differ from a plain program's by a relative error of at most 0.0049.
Values may be sent and summed in bfloat16 or wider, within the bound.
No kernel may reach another device: no remote copies, remote signals or barrier semaphores. Data moves between devices by JAX's collectives and lax.ppermute only.
A program may use at most 64 MiB of HBM per device.

v0:
```python
import jax
import jax.numpy as jnp
from jax import lax
from jax.sharding import PartitionSpec as P


def tensor_sum(partial_value, tensor_count):
    position = lax.axis_index("tensor")
    block = partial_value
    steps = []
    step = 1
    while step < tensor_count:
        half = block.shape[0] // 2
        upper = position // step % 2
        low_part = block[:half]
        high_part = block[half:]
        keep = jnp.where(upper == 1, high_part, low_part)
        send = jnp.where(upper == 1, low_part, high_part)
        exchange = [(i, i ^ step) for i in range(tensor_count)]
        block = keep + lax.ppermute(send, "tensor", exchange)
        steps.append((step, upper))
        step *= 2
    block = block.astype(jnp.bfloat16)
    for step, upper in reversed(steps):
        exchange = [(i, i ^ step) for i in range(tensor_count)]
        other = lax.ppermute(block, "tensor", exchange)
        block = jnp.where(
            upper == 1,
            jnp.concatenate([other, block], axis=0),
            jnp.concatenate([block, other], axis=0),
        )
    return block


def body(
    tokens,
    key_value_weight,
    adapter_down_maps,
    adapter_up_maps,
    adapter_per_row,
    adapter_storage_slot,
):
    row_count, feature_portion = tokens.shape
    wide_count = lax.axis_size("wide")
    tensor_count = lax.axis_size("tensor")
    capacity = 2 * row_count // wide_count
    present_adapters = adapter_down_maps.shape[1]
    rank_dimension = adapter_down_maps.shape[2]
    column_portion = key_value_weight.shape[1]
    total_adapters = adapter_storage_slot.shape[0]
    slot_count = wide_count * capacity
    lane = 128
    row_tiles = capacity * feature_portion // lane
    info_rows = 8
    gathered = lax.all_gather(tokens, "tensor", axis=1, tiled=True)
    base_projection_output = jnp.dot(gathered, key_value_weight, preferred_element_type=jnp.float32)
    adapter_match = adapter_per_row[:, None] == jnp.arange(total_adapters, dtype=jnp.int32)[None, :]
    storage_position = jnp.sum(jnp.where(adapter_match, adapter_storage_slot[None, :], 0), axis=1)
    owner_index = storage_position // present_adapters
    local_index = storage_position % present_adapters
    owner_onehot = (
        owner_index[:, None] == jnp.arange(wide_count, dtype=jnp.int32)[None, :]
    ).astype(jnp.float32)
    row_iota = jnp.arange(row_count, dtype=jnp.int32)
    strictly_before = (row_iota[:, None] > row_iota[None, :]).astype(jnp.float32)
    earlier = jnp.dot(strictly_before, owner_onehot, preferred_element_type=jnp.float32)
    rank_in_owner = jnp.sum(earlier * owner_onehot, axis=1).astype(jnp.int32)
    destination = owner_index * capacity + rank_in_owner
    placement = (jnp.arange(slot_count, dtype=jnp.int32)[:, None] == destination[None, :]).astype(
        jnp.bfloat16
    )
    local_code = jnp.broadcast_to(
        (local_index + 1).astype(jnp.bfloat16)[:, None], (row_count, lane)
    )
    extended = jnp.concatenate([tokens, local_code], axis=1)
    placed = jnp.dot(placement, extended, preferred_element_type=jnp.float32).astype(jnp.bfloat16)
    send_rows = placed[:, :feature_portion].reshape(wide_count, row_tiles, lane)
    slot_code = placed[:, feature_portion].reshape(wide_count, 1, capacity)
    slot_code = jnp.pad(slot_code, ((0, 0), (0, info_rows - 1), (0, lane - capacity)))
    send_block = jnp.concatenate([send_rows, slot_code], axis=1)
    got_block = lax.all_to_all(send_block, "wide", split_axis=0, concat_axis=0, tiled=True)
    flat_rows = got_block[:, :row_tiles, :].reshape(slot_count, feature_portion)
    got_code = got_block[:, row_tiles, :capacity].reshape(slot_count).astype(jnp.int32)
    selected = (got_code[:, None] == jnp.arange(1, present_adapters + 1, dtype=jnp.int32)[None, :])[
        :, :, None
    ]
    down_matrix = adapter_down_maps.reshape(feature_portion, present_adapters * rank_dimension)
    all_ranks = jnp.dot(flat_rows, down_matrix, preferred_element_type=jnp.float32)
    all_ranks = all_ranks.reshape(slot_count, present_adapters, rank_dimension)
    partial_value = jnp.sum(jnp.where(selected, all_ranks, 0.0), axis=1)
    ordered = partial_value + 0.0 * gathered[0, 0].astype(jnp.float32)
    scattered = lax.psum_scatter(ordered, "tensor", scatter_dimension=0, tiled=True)
    wide_block = jnp.pad(scattered.astype(jnp.bfloat16), ((0, 0), (0, 448)))
    reduced_rows = lax.all_gather(wide_block, "tensor", axis=0, tiled=True)[:, :64]
    expanded_rows = jnp.where(
        selected, reduced_rows[:, None, :], jnp.zeros((), jnp.bfloat16)
    ).reshape(slot_count, present_adapters * rank_dimension)
    up_matrix = adapter_up_maps.reshape(present_adapters * rank_dimension, column_portion)
    adapter_correction = jnp.dot(
        expanded_rows, up_matrix, preferred_element_type=jnp.float32
    ).astype(jnp.bfloat16)
    adapter_correction = adapter_correction.reshape(wide_count, capacity, column_portion)
    returned_rows = lax.all_to_all(
        adapter_correction, "wide", split_axis=0, concat_axis=0, tiled=True
    )
    returned_rows = returned_rows.reshape(slot_count, column_portion)
    adapter_row_output = jnp.dot(placement.T, returned_rows, preferred_element_type=jnp.float32)
    return (base_projection_output + adapter_row_output).astype(jnp.bfloat16)


def solution(mesh):
    in_specs = (
        P("wide", "tensor"),
        P(None, "tensor"),
        P("tensor", "wide", None),
        P("wide", None, "tensor"),
        P("wide"),
        P(),
    )
    out_specs = P("wide", "tensor")
    return jax.shard_map(body, mesh=mesh, in_specs=in_specs, out_specs=out_specs, check_vma=False)
```

profile of v0, /device:TPU:8, one launch (start us, length us, event | category | flops | bytes accessed | tf_op | source)
XLA Modules:
  0.0 209.3 jit_solution(6343781459754959343)
XLA Ops:
  6.5 0.0 copy-start
  6.5 0.0 all-gather.3.cloned.1.call-start
  6.5 0.7 all-gather.3.cloned.1.call-update
  7.3 0.9 select_reduce_fusion.1
  8.2 0.3 fusion.15
  8.5 0.1 broadcast_in_dim.39
  8.7 2.0 fusion.6
  10.6 0.0 copy-start.1
  10.6 1.2 copy-done.1
  11.8 0.1 slice.24
  11.9 1.3 copy.14
  13.2 1.7 reshape.117
  14.9 0.7 slice_reduce_fusion
  15.6 0.1 reshape_squeeze.5
  15.7 1.2 fusion.16
  16.9 13.2 %all-to-all-start = ((bf16[32,136,128]{2,1,0:T(8,128)(2,1)}), bf16[32,136,128]{2,1,0:T(8,128)(2,1)S(1)}, u32[]{:S(2)}, u32[]{:S(2)}) async-start(bf16[32,136,128]{2,1,0:T(8,128)(2,1)} %fusion.16), calls=%async_computation | async-start | bytes 2228224 | tf_op jit(solution)/shard_map/all_to_all | solution.py:81
  30.1 0.0 reduce-scatter.4.cloned.1.call-start
  30.1 29.4 %all-to-all-done = bf16[32,136,128]{2,1,0:T(8,128)(2,1)S(1)} async-done(((bf16[32,136,128]{2,1,0:T(8,128)(2,1)}), bf16[32,136,128]{2,1,0:T(8,128)(2,1)S(1)}, u32[]{:S(2)}, u32[]{:S(2)}) %all-to-all-start) | async-done | bytes 1114144 | tf_op jit(solution)/shard_map/all_to_all | solution.py:81
  59.5 0.1 fusion.26
  59.6 0.1 reshape.122
  59.6 1.2 slice.27
  60.8 1.7 reshape.123
  62.6 0.1 broadcast_compare_fusion
  62.6 2.6 %select_reduce_fusion = f32[1024,64]{0,1:T(8,128)S(1)} fusion(bf16[1024,512,1]{1,0,2:T(8,128)(2,1)S(1)} %reshape.123, pred[1024,16]{0,1:T(8,128)(4,1)S(1)} %broadcast_compare_fusion, bf16[512,16,64]{0,2,1:T(8,128)(2,1)} %param.8), kind=kOutput, calls=%fused_computation | convolution fusion | flops 1075773440 | bytes 2375680 | tf_op jit(solution)/shard_map/dot_general | solution.py:88
  65.2 0.0 copy-start.2
  65.2 5.7 %all-gather.3.cloned.1.call-done = bf16[512,8192]{1,0:T(8,128)(2,1)} async-done(((bf16[512,512]{1,0:T(8,128)(2,1)}), bf16[512,8192]{1,0:T(8,128)(2,1)}) %all-gather.3.cloned.1.call-update) | async-done | bytes 8388624 | tf_op jit(solution)/shard_map/all_gather | solution.py:55
  70.9 1.2 slice.28
  72.8 1.1 copy.18
  73.8 0.0 reduce-scatter.4.cloned.1.call-update
  73.9 0.0 all-gather.5.cloned.1.call-start
  73.9 56.4 %reduce-scatter.4.cloned.1.call-done = f32[64,64]{1,0:T(8,128)} async-done(((f32[1024,64]{1,0:T(8,128)}), f32[64,64]{1,0:T(8,128)}) %reduce-scatter.4.cloned.1.call-update) | async-done | bytes 16400
  130.3 0.8 copy.19
  131.2 0.1 copy.20
  131.3 0.7 pad.9.clone
  131.9 0.0 all-gather.5.cloned.1.call-update
  131.9 43.3 %all-gather.5.cloned.1.call-done = bf16[1024,512]{1,0:T(8,128)(2,1)} async-done(((bf16[64,512]{1,0:T(8,128)(2,1)}), bf16[1024,512]{1,0:T(8,128)(2,1)}) %all-gather.5.cloned.1.call-update) | async-done | bytes 1048592 | tf_op jit(solution)/shard_map/all_gather | solution.py:94
  175.2 1.0 slice.29
  176.2 0.1 copy.17
  176.3 0.0 copy-done.2
  176.3 1.5 fusion.10
  177.8 10.2 %all-to-all-start.1 = ((bf16[32,32,128]{2,1,0:T(8,128)(2,1)}), bf16[32,32,128]{2,1,0:T(8,128)(2,1)S(1)}, u32[]{:S(2)}, u32[]{:S(2)}) async-start(bf16[32,32,128]{2,1,0:T(8,128)(2,1)} %bitcast.5), calls=%async_computation.1 | async-start | bytes 524288 | tf_op jit(solution)/shard_map/all_to_all | solution.py:103
  188.0 0.0 copy-done
  188.0 5.7 %fusion.32 = f32[512,128]{1,0:T(8,128)S(1)} fusion(bf16[512,8192]{1,0:T(8,128)(2,1)} %all-gather.3.cloned.1.call-done, bf16[8192,128]{1,0:T(8,128)(2,1)S(1)} %copy-done), kind=kOutput, calls=%fused_computation.49 | convolution fusion | flops 1073741824 | bytes 10747904 | tf_op jit(solution)/shard_map/dot_general | solution.py:56
  193.7 7.7 %all-to-all-done.1 = bf16[32,32,128]{2,1,0:T(8,128)(2,1)S(1)} async-done(((bf16[32,32,128]{2,1,0:T(8,128)(2,1)}), bf16[32,32,128]{2,1,0:T(8,128)(2,1)S(1)}, u32[]{:S(2)}, u32[]{:S(2)}) %all-to-all-start.1) | async-done | bytes 262176 | tf_op jit(solution)/shard_map/all_to_all | solution.py:103
  201.4 1.4 fusion.14
  (4 shorter events, 0.0 us)
Async XLA Ops:
  6.5 181.5 %copy-start = (bf16[8192,128]{1,0:T(8,128)(2,1)S(1)}, bf16[8192,128]{1,0:T(8,128)(2,1)}, u32[]{:S(2)}) copy-start(bf16[8192,128]{1,0:T(8,128)(2,1)} %param.7) | copy-start | bytes 6291460
  6.5 64.4 %all-gather.3.cloned.1.call-start = ((), (), s32[]{:S(2)}) async-start(), calls=%async_computation.3 | async-start | bytes 8912896 | tf_op jit(solution)/shard_map/all_gather | solution.py:55
  10.6 1.2 copy-start.1
  16.9 42.6 %all-to-all-start = ((bf16[32,136,128]{2,1,0:T(8,128)(2,1)}), bf16[32,136,128]{2,1,0:T(8,128)(2,1)S(1)}, u32[]{:S(2)}, u32[]{:S(2)}) async-start(bf16[32,136,128]{2,1,0:T(8,128)(2,1)} %fusion.16), calls=%async_computation | async-start | bytes 2228224 | tf_op jit(solution)/shard_map/all_to_all | solution.py:81
  30.1 100.2 %reduce-scatter.4.cloned.1.call-start = ((), (), s32[]{:S(2)}) async-start(), calls=%async_computation.5 | async-start | bytes 557056
  65.2 111.1 %copy-start.2 = (bf16[16,64,128]{2,1,0:T(8,128)(2,1)S(1)}, bf16[16,64,128]{2,1,0:T(8,128)(2,1)}, u32[]{:S(2)}) copy-start(bf16[16,64,128]{2,1,0:T(8,128)(2,1)} %param.9) | copy-start | bytes 786436
  73.9 101.3 %all-gather.5.cloned.1.call-start = ((), (), s32[]{:S(2)}) async-start(), calls=%async_computation.4 | async-start | bytes 1114112 | tf_op jit(solution)/shard_map/all_gather | solution.py:94
  177.8 23.6 %all-to-all-start.1 = ((bf16[32,32,128]{2,1,0:T(8,128)(2,1)}), bf16[32,32,128]{2,1,0:T(8,128)(2,1)S(1)}, u32[]{:S(2)}, u32[]{:S(2)}) async-start(bf16[32,32,128]{2,1,0:T(8,128)(2,1)} %bitcast.5), calls=%async_computation.1 | async-start | bytes 524288 | tf_op jit(solution)/shard_map/all_to_all | solution.py:103
Sparse Core Ops, SparseCore 0:
  9.5 61.3 all-gather.2
  74.0 56.2 reduce-scatter.3
  132.7 42.4 all-gather.4
where the time goes:
time: 210 us; the launch traced here: 209 us
  waiting for transfers between devices  143 us (68%)
  starting transfers between devices  23.4 us (11%)
  between operations  13.9 us (7%)
  matrix products  13.4 us (6%)
  local copies, waits for them, and re-layouts  13.1 us (6%)
  other arithmetic  2.31 us (1%)
    unnamed x4, waiting for transfers between devices  57.2 us
    all_gather x1, waiting for transfers between devices, body(): lax.all_gather(wide_block, 'tensor', axis=0, tiled=True)[:, :64]  43.3 us
    all_to_all x1, waiting for transfers between devices, body(): lax.all_to_all(send_block, 'wide', split_axis=0, concat_axis=0, tiled=True)  29.4 us
    all_to_all x1, starting transfers between devices, body(): lax.all_to_all(send_block, 'wide', split_axis=0, concat_axis=0, tiled=True)  13.2 us
    all_to_all x1, starting transfers between devices, body(): lax.all_to_all(adapter_correction, 'wide', split_axis=0, concat_axis=0, t...  10.2 us
    all_to_all x1, waiting for transfers between devices, body(): lax.all_to_all(adapter_correction, 'wide', split_axis=0, concat_axis=0, t...  7.66 us
    dot_general x1, matrix products, body(): jnp.dot(gathered, key_value_weight, preferred_element_type=jnp.float32)  5.7 us
    all_gather x1, waiting for transfers between devices, body(): gathered = lax.all_gather(tokens, 'tensor', axis=1, tiled=True)  5.69 us
  transfers between devices with their start and end apart: 5, of which 5 were waited for; matrix products, arithmetic and copies ran while one was open for 9% of the time, Pallas kernels for 0%

commit v1 on v0

--- a/solution.py
+++ b/solution.py
@@ -2,6 +2,7 @@
 import jax.numpy as jnp
 from jax import lax
 from jax.sharding import PartitionSpec as P
+from jax.lax import all_to_all, axis_size
 
 
 def tensor_sum(partial_value, tensor_count):
@@ -91,7 +92,18 @@
     ordered = partial_value + 0.0 * gathered[0, 0].astype(jnp.float32)
     scattered = lax.psum_scatter(ordered, "tensor", scatter_dimension=0, tiled=True)
     wide_block = jnp.pad(scattered.astype(jnp.bfloat16), ((0, 0), (0, 448)))
-    reduced_rows = lax.all_gather(wide_block, "tensor", axis=0, tiled=True)[:, :64]
+
+    def number_lanes(chunk):
+        axis_len = axis_size("tensor")
+        return all_to_all(
+            jnp.tile(chunk, [axis_len if j0 == 0 else 1 for j0 in range(chunk.ndim)]),
+            axis_name="tensor",
+            split_axis=0,
+            concat_axis=0,
+            tiled=True,
+        )
+
+    reduced_rows = number_lanes(wide_block)[:, :64]
     expanded_rows = jnp.where(
         selected, reduced_rows[:, None, :], jnp.zeros((), jnp.bfloat16)
     ).reshape(slot_count, present_adapters * rank_dimension)

time: 210 us -> 202 us (0.962)
  the two profiles are of different devices: /device:TPU:8 before, /device:TPU:1 now
where the time goes in v1:
time: 202 us; the launch traced here: 201 us
  waiting for transfers between devices  101 us (50%)
  blocking collectives  35.2 us (17%)
  starting transfers between devices  23.7 us (12%)
  between operations  14.2 us (7%)
  matrix products  13.4 us (7%)
  local copies, waits for them, and re-layouts  11.7 us (6%)
  other arithmetic  2.31 us (1%)
    unnamed x3, waiting for transfers between devices  56.7 us
    all_to_all x1, blocking collectives, number_lanes(): all_to_all(jnp.tile(chunk, [axis_len if j0 == 0 else 1 for j0 in range(ch...  35.2 us
    all_to_all x1, waiting for transfers between devices, body(): lax.all_to_all(send_block, 'wide', split_axis=0, concat_axis=0, tiled=True)  27.3 us
    all_to_all x1, starting transfers between devices, body(): lax.all_to_all(send_block, 'wide', split_axis=0, concat_axis=0, tiled=True)  13.7 us
    all_gather x1, waiting for transfers between devices, body(): gathered = lax.all_gather(tokens, 'tensor', axis=1, tiled=True)  9.95 us
    all_to_all x1, starting transfers between devices, body(): lax.all_to_all(adapter_correction, 'wide', split_axis=0, concat_axis=0, t...  9.9 us
    all_to_all x1, waiting for transfers between devices, body(): lax.all_to_all(adapter_correction, 'wide', split_axis=0, concat_axis=0, t...  6.98 us
    dot_general x1, matrix products, body(): jnp.dot(gathered, key_value_weight, preferred_element_type=jnp.float32)  5.7 us
  transfers between devices with their start and end apart: 4, of which 4 were waited for; matrix products, arithmetic and copies ran while one was open for 10% of the time, Pallas kernels for 0%

profile of v1, /device:TPU:1, one launch (start us, length us, event | category | flops | bytes accessed | tf_op | source)
XLA Modules:
  0.0 201.3 jit_solution(17393839653652171530)
XLA Ops:
  6.5 0.0 copy-start
  6.5 0.0 all-gather.2.cloned.1.call-start
  6.5 0.7 all-gather.2.cloned.1.call-update
  7.3 0.9 select_reduce_fusion.1
  8.2 0.3 fusion.15
  8.5 0.1 broadcast_in_dim.39
  8.7 2.0 fusion.6
  10.6 0.0 copy-start.1
  10.6 1.2 copy-done.1
  11.8 0.1 slice.24
  11.9 1.3 copy.19
  13.2 1.7 reshape.124
  14.9 0.7 slice_reduce_fusion
  15.6 0.1 reshape_squeeze.5
  15.7 1.2 fusion.16
  16.9 13.7 %all-to-all-start = ((bf16[32,136,128]{2,1,0:T(8,128)(2,1)}), bf16[32,136,128]{2,1,0:T(8,128)(2,1)S(1)}, u32[]{:S(2)}, u32[]{:S(2)}) async-start(bf16[32,136,128]{2,1,0:T(8,128)(2,1)} %fusion.16), calls=%async_computation | async-start | bytes 2228224 | tf_op jit(solution)/shard_map/all_to_all | solution.py:82
  30.6 0.0 reduce-scatter.4.cloned.1.call-start
  30.7 27.3 %all-to-all-done = bf16[32,136,128]{2,1,0:T(8,128)(2,1)S(1)} async-done(((bf16[32,136,128]{2,1,0:T(8,128)(2,1)}), bf16[32,136,128]{2,1,0:T(8,128)(2,1)S(1)}, u32[]{:S(2)}, u32[]{:S(2)}) %all-to-all-start) | async-done | bytes 1114144 | tf_op jit(solution)/shard_map/all_to_all | solution.py:82
  58.0 0.1 fusion.26
  58.0 0.1 reshape.129
  58.1 1.2 slice.27
  59.3 1.8 reshape.130
  61.1 0.1 broadcast_compare_fusion
  61.2 2.5 %select_reduce_fusion = f32[1024,64]{0,1:T(8,128)S(1)} fusion(bf16[1024,512,1]{1,0,2:T(8,128)(2,1)S(1)} %reshape.130, pred[1024,16]{0,1:T(8,128)(4,1)S(1)} %broadcast_compare_fusion, bf16[512,16,64]{0,2,1:T(8,128)(2,1)} %param.8), kind=kOutput, calls=%fused_computation | convolution fusion | flops 1075773440 | bytes 2375680 | tf_op jit(solution)/shard_map/dot_general | solution.py:89
  63.7 10.0 %all-gather.2.cloned.1.call-done = bf16[512,8192]{1,0:T(8,128)(2,1)} async-done(((bf16[512,512]{1,0:T(8,128)(2,1)}), bf16[512,8192]{1,0:T(8,128)(2,1)}) %all-gather.2.cloned.1.call-update) | async-done | bytes 8388624 | tf_op jit(solution)/shard_map/all_gather | solution.py:56
  73.7 1.2 slice.28
  75.5 1.1 copy.23
  76.6 0.0 reduce-scatter.4.cloned.1.call-update
  76.6 55.9 %reduce-scatter.4.cloned.1.call-done = f32[64,64]{1,0:T(8,128)} async-done(((f32[1024,64]{1,0:T(8,128)}), f32[64,64]{1,0:T(8,128)}) %reduce-scatter.4.cloned.1.call-update) | async-done | bytes 16400
  132.6 0.8 copy.24
  133.4 0.1 copy.25
  133.5 0.0 copy-start.2
  133.5 0.1 tile.2
  133.6 35.2 %all_to_all.19 = bf16[16,64,512]{2,1,0:T(8,128)(2,1)S(1)} all-to-all(bf16[16,64,512]{2,1,0:T(8,128)(2,1)S(1)} %tile.2), channel_id=1, replica_groups=mesh['wide'=32,'tensor'=16] {'tensor'}, dimensions={0} | all-to-all | bytes 2097152 | tf_op jit(solution)/shard_map/all_to_all | solution.py:98
  168.8 0.1 copy.22
  169.0 0.0 copy-done.2
  169.0 1.5 fusion.10
  170.5 9.9 %all-to-all-start.2 = ((bf16[32,32,128]{2,1,0:T(8,128)(2,1)}), bf16[32,32,128]{2,1,0:T(8,128)(2,1)S(1)}, u32[]{:S(2)}, u32[]{:S(2)}) async-start(bf16[32,32,128]{2,1,0:T(8,128)(2,1)} %bitcast.6), calls=%async_computation.2 | async-start | bytes 524288 | tf_op jit(solution)/shard_map/all_to_all | solution.py:115
  180.4 0.0 copy-done
  180.4 5.7 %fusion.32 = f32[512,128]{1,0:T(8,128)S(1)} fusion(bf16[512,8192]{1,0:T(8,128)(2,1)} %all-gather.2.cloned.1.call-done, bf16[8192,128]{1,0:T(8,128)(2,1)S(1)} %copy-done), kind=kOutput, calls=%fused_computation.49 | convolution fusion | flops 1073741824 | bytes 10747904 | tf_op jit(solution)/shard_map/dot_general | solution.py:57
  186.1 7.0 %all-to-all-done.2 = bf16[32,32,128]{2,1,0:T(8,128)(2,1)S(1)} async-done(((bf16[32,32,128]{2,1,0:T(8,128)(2,1)}), bf16[32,32,128]{2,1,0:T(8,128)(2,1)S(1)}, u32[]{:S(2)}, u32[]{:S(2)}) %all-to-all-start.2) | async-done | bytes 262176 | tf_op jit(solution)/shard_map/all_to_all | solution.py:115
  193.1 1.4 fusion.14
  (6 shorter events, 0.1 us)
Async XLA Ops:
  6.5 173.8 %copy-start = (bf16[8192,128]{1,0:T(8,128)(2,1)S(1)}, bf16[8192,128]{1,0:T(8,128)(2,1)}, u32[]{:S(2)}) copy-start(bf16[8192,128]{1,0:T(8,128)(2,1)} %param.7) | copy-start | bytes 6291460
  6.5 67.1 %all-gather.2.cloned.1.call-start = ((), (), s32[]{:S(2)}) async-start(), calls=%async_computation.4 | async-start | bytes 8912896 | tf_op jit(solution)/shard_map/all_gather | solution.py:56
  10.6 1.2 copy-start.1
  16.9 41.1 %all-to-all-start = ((bf16[32,136,128]{2,1,0:T(8,128)(2,1)}), bf16[32,136,128]{2,1,0:T(8,128)(2,1)S(1)}, u32[]{:S(2)}, u32[]{:S(2)}) async-start(bf16[32,136,128]{2,1,0:T(8,128)(2,1)} %fusion.16), calls=%async_computation | async-start | bytes 2228224 | tf_op jit(solution)/shard_map/all_to_all | solution.py:82
  30.6 101.9 %reduce-scatter.4.cloned.1.call-start = ((), (), s32[]{:S(2)}) async-start(), calls=%async_computation.5 | async-start | bytes 557056
  133.5 35.5 %copy-start.2 = (bf16[16,64,128]{2,1,0:T(8,128)(2,1)S(1)}, bf16[16,64,128]{2,1,0:T(8,128)(2,1)}, u32[]{:S(2)}) copy-start(bf16[16,64,128]{2,1,0:T(8,128)(2,1)} %param.9) | copy-start | bytes 786436
  170.5 22.6 %all-to-all-start.2 = ((bf16[32,32,128]{2,1,0:T(8,128)(2,1)}), bf16[32,32,128]{2,1,0:T(8,128)(2,1)S(1)}, u32[]{:S(2)}, u32[]{:S(2)}) async-start(bf16[32,32,128]{2,1,0:T(8,128)(2,1)} %bitcast.6), calls=%async_computation.2 | async-start | bytes 524288 | tf_op jit(solution)/shard_map/all_to_all | solution.py:115
Sparse Core Ops, SparseCore 0:
  9.5 64.1 all-gather.1
  76.7 55.7 reduce-scatter.3
